TPU v7x, 32 devices: a whole 2x2x4 slice. The times are simulated.
32 devices in a mesh: ctx: 8 (over z, x), dp: 4 (over y, core).
Axes of the slice: x: 2, y: 2, z: 4, core: 2. Of those that a mesh axis runs over, the one named last changes fastest.
Arguments:
- queries: bfloat16 [4, 2048, 512], P('dp', 'ctx'), may hold values from -3 to 3
- keys: bfloat16 [4, 2048, 512], P('dp', 'ctx'), may hold values from -6 to 6
- values: bfloat16 [4, 2048, 512], P('dp', 'ctx'), may hold values from -6 to 6
- gates: bfloat16 [4, 2048, 512], P('dp', 'ctx'), may hold values from -6 to 6
- out_grad: bfloat16 [4, 2048, 512], P('dp', 'ctx'), may hold values from -6 to 6
- time_bucket: int32 [4, 2048], P('dp'), may hold values from 0 to 127
- lengths: int32 [4, 6], P('dp'), may hold values from 1 to 1024, 2048 in all within a row
- block_map: int32 [4, 16, 16], P('dp'), may hold values 0 or 1
- bucket_bias_matrix: bfloat16 [4, 128, 128], replicated, may hold values from 1 to 3
- w_out: bfloat16 [512, 512], replicated, may hold values from -0.25 to 0.25
Outputs:
- query_grad: bfloat16 [4, 2048, 512], P('dp', 'ctx')
- key_grad: bfloat16 [4, 2048, 512], P('dp', 'ctx')
- value_grad: bfloat16 [4, 2048, 512], P('dp', 'ctx')
- gate_grad: bfloat16 [4, 2048, 512], P('dp', 'ctx')
- w_out_grad: float32 [512, 512], P('dp')
- table_grad: float32 [4, 128, 128], replicated
Inputs may be any that keep to these rules, and one draw needn't show every extreme that they name: Each row of lengths sums to 2048, and its largest entry is 1024. `block_map`: 1 marks a visible pair of blocks.
All inputs are finite; a program needn't handle non-finite values.
Results may differ from a plain program's by a relative error of at most 0.0059.
Values may be sent and summed in bfloat16 or wider, within the bound.
No kernel may reach another device: no remote copies, remote signals or barrier semaphores. Data moves between devices by JAX's collectives and lax.ppermute only.
A program may use at most 64 MiB of HBM per device.

v0:
```python
import jax
import jax.numpy as jnp
from jax import lax
from jax.sharding import PartitionSpec as P

BLK = 128
NORM_EPSILON = 1e-05


def passed_along(value, axis, by):
    length = lax.axis_size(axis)
    pairs = [(i, i + by) for i in range(length) if 0 <= i + by < length]
    return lax.ppermute(value, axis, pairs)


def silu_slope(scores):
    sigmoid = jax.nn.sigmoid(scores)
    return sigmoid * (1.0 + scores * (1.0 - sigmoid))


def expand_blocks(block_rows, block_size):
    return jnp.repeat(jnp.repeat(block_rows, block_size, axis=0), block_size, axis=1)


def shards(
    queries,
    keys,
    values,
    gates,
    out_grad,
    time_bucket,
    lengths,
    block_map,
    bucket_bias_matrix,
    w_out,
):
    query_rows = queries[0]
    key_rows = keys[0]
    value_rows = values[0]
    gate_rows = gates[0]
    grad_rows = out_grad[0]
    local_rows, width = query_rows.shape
    head_count = bucket_bias_matrix.shape[0]
    bucket_count = bucket_bias_matrix.shape[1]
    head_dim = width // head_count
    scale = head_dim ** (-0.5)
    blocks_here = local_rows // BLK
    cycle_index = lax.axis_index("ctx")
    row_start = cycle_index * local_rows
    offsets = jnp.cumsum(lengths[0], dtype=jnp.int32) - lengths[0]

    def segment_of(positions):
        return jnp.sum(
            (positions[:, None] >= offsets[None, 1:]).astype(jnp.int32), axis=1, dtype=jnp.int32
        )

    bucket_ids = jnp.arange(bucket_count, dtype=jnp.int32)
    query_pos = row_start + jnp.arange(local_rows, dtype=jnp.int32)
    query_seg = segment_of(query_pos)
    query_bucket = lax.dynamic_slice_in_dim(time_bucket[0], row_start, local_rows, 0)
    query_bucket_indicator = (query_bucket[:, None] == bucket_ids[None, :]).astype(jnp.bfloat16)
    bias_matrix_rows = jnp.einsum(
        "lf,sfq->slq",
        query_bucket_indicator,
        bucket_bias_matrix,
        preferred_element_type=jnp.float32,
    ).astype(jnp.bfloat16)
    map_rows = lax.dynamic_slice_in_dim(block_map[0], cycle_index * blocks_here, blocks_here, 0)
    query_heads = query_rows.reshape(local_rows, head_count, head_dim)
    stacked = jnp.stack([key_rows, value_rows])
    window = [stacked, passed_along(stacked, "ctx", 1), passed_along(stacked, "ctx", 2)]
    tiles = []
    attended = jnp.zeros((local_rows, head_count, head_dim), jnp.float32)
    for distance in range(3):
        key_first = row_start - distance * local_rows
        key_pos = key_first + jnp.arange(local_rows, dtype=jnp.int32)
        safe_first = jnp.maximum(key_first, 0)
        key_bucket = lax.dynamic_slice_in_dim(time_bucket[0], safe_first, local_rows, 0)
        key_bucket_indicator = (key_bucket[:, None] == bucket_ids[None, :]).astype(jnp.bfloat16)
        map_cols = lax.dynamic_slice_in_dim(map_rows, safe_first // BLK, blocks_here, 1)
        same_block = query_pos[:, None] // BLK == key_pos[None, :] // BLK
        key_visible = (
            (query_seg[:, None] == segment_of(key_pos)[None, :])
            & (key_pos[None, :] <= query_pos[:, None])
            & (key_pos[None, :] >= 0)
            & ((expand_blocks(map_cols, BLK) == 1) | same_block)
        )
        key_bias_terms = jnp.einsum(
            "vqx,px->vqp",
            bias_matrix_rows,
            key_bucket_indicator,
            preferred_element_type=jnp.float32,
        )
        visible, bias_terms, key_bucket_indicator = (
            key_visible,
            key_bias_terms,
            key_bucket_indicator,
        )
        forward_pair = window[distance]
        forward_key_heads = forward_pair[0].reshape(local_rows, head_count, head_dim)
        forward_value_heads = forward_pair[1].reshape(local_rows, head_count, head_dim)
        forward_scores = (
            jnp.einsum(
                "ihd,jhd->hij", query_heads, forward_key_heads, preferred_element_type=jnp.float32
            )
            * scale
            + bias_terms
        )
        forward_weights = jnp.where(visible[None], jax.nn.silu(forward_scores), 0.0).astype(
            jnp.bfloat16
        )
        attended_part = jnp.einsum(
            "hij,jhd->ihd", forward_weights, forward_value_heads, preferred_element_type=jnp.float32
        )
        attended = attended + attended_part
        tiles.append((visible, forward_scores, forward_weights, key_bucket_indicator))
    attended = attended.reshape(local_rows, width)
    centered = attended - jnp.mean(attended, axis=1, keepdims=True)
    inverse = lax.rsqrt(jnp.mean(centered * centered, axis=1, keepdims=True) + NORM_EPSILON)
    normed = centered * inverse
    dz_rows = lax.dot_general(
        grad_rows, w_out, (((1,), (1,)), ((), ())), preferred_element_type=jnp.float32
    )
    gate_float = gate_rows.astype(jnp.float32)
    gate_grad = (dz_rows * normed).astype(jnp.bfloat16)
    mixed = (normed * gate_float).astype(jnp.bfloat16)
    lifted = dz_rows * gate_float
    attended_grad = (
        (
            lifted
            - jnp.mean(lifted, axis=1, keepdims=True)
            - normed * jnp.mean(lifted * normed, axis=1, keepdims=True)
        )
        * inverse
    ).astype(jnp.bfloat16)
    grad_heads = attended_grad.reshape(local_rows, head_count, head_dim)
    indicator_float = query_bucket_indicator.astype(jnp.float32)
    query_sum = jnp.zeros((local_rows, width), jnp.float32)
    table_local = jnp.zeros((head_count, bucket_count, bucket_count), jnp.float32)
    key_terms = []
    for distance in range(3):
        visible, scores, weights, key_bucket_indicator = tiles[distance]
        pair = window[distance]
        key_heads = pair[0].reshape(local_rows, head_count, head_dim)
        value_heads = pair[1].reshape(local_rows, head_count, head_dim)
        weight_grad = jnp.einsum(
            "ihd,jhd->hij", grad_heads, value_heads, preferred_element_type=jnp.float32
        )
        value_part = jnp.einsum(
            "hij,ihd->jhd", weights, grad_heads, preferred_element_type=jnp.float32
        ).reshape(local_rows, width)
        score_gradient = jnp.where(visible[None], weight_grad * silu_slope(scores), 0.0).astype(
            jnp.bfloat16
        )
        query_part = jnp.einsum(
            "hij,jhd->ihd", score_gradient, key_heads, preferred_element_type=jnp.float32
        ).reshape(local_rows, width)
        key_part = (
            jnp.einsum(
                "hij,ihd->jhd", score_gradient, query_heads, preferred_element_type=jnp.float32
            ).reshape(local_rows, width)
            * scale
        )
        bucket_share_piece = jnp.einsum(
            "rmw,wx->rmx", score_gradient, key_bucket_indicator, preferred_element_type=jnp.float32
        )
        table_part = jnp.einsum(
            "qp,cqk->cpk", indicator_float, bucket_share_piece, precision=lax.Precision.HIGHEST
        )
        query_sum = query_sum + query_part
        table_local = table_local + table_part
        key_terms.append(jnp.stack([key_part, value_part]))
    gathered = (
        key_terms[0] + passed_along(key_terms[1], "ctx", -1) + passed_along(key_terms[2], "ctx", -2)
    )
    query_grad = (query_sum * scale).astype(jnp.bfloat16)
    key_grad = gathered[0].astype(jnp.bfloat16)
    value_grad = gathered[1].astype(jnp.bfloat16)
    weight_rows = lax.psum_scatter(
        lax.dot_general(
            mixed, grad_rows, (((0,), (0,)), ((), ())), preferred_element_type=jnp.float32
        ),
        "dp",
        scatter_dimension=0,
        tiled=True,
    )
    projection_grad = lax.psum(weight_rows, "ctx")
    table_grad = lax.psum(table_local, ("ctx", "dp"))
    return (
        query_grad[None],
        key_grad[None],
        value_grad[None],
        gate_grad[None],
        projection_grad,
        table_grad,
    )


def solution(mesh):
    return jax.shard_map(
        shards,
        mesh=mesh,
        in_specs=(
            P("dp", "ctx", None),
            P("dp", "ctx", None),
            P("dp", "ctx", None),
            P("dp", "ctx", None),
            P("dp", "ctx", None),
            P("dp", None),
            P("dp", None),
            P("dp", None, None),
            P(),
            P(),
        ),
        out_specs=(
            P("dp", "ctx", None),
            P("dp", "ctx", None),
            P("dp", "ctx", None),
            P("dp", "ctx", None),
            P("dp", None),
            P(),
        ),
        check_vma=False,
    )
```

profile of v0, /device:TPU:0, one launch (start us, length us, event | category | flops | bytes accessed | tf_op | source)
XLA Modules:
  0.0 265.2 jit_solution(2168080147234761298)
XLA Ops:
  8.1 1.2 copy.148
  10.2 5.8 %collective-permute-start.1 = (bf16[2,256,512]{1,2,0:T(8,128)(2,1)}, bf16[2,256,512]{1,2,0:T(8,128)(2,1)}, u32[]{:S(2)}, u32[]{:S(2)}) collective-permute-start(bf16[2,256,512]{1,2,0:T(8,128)(2,1)} %pad_maximum_fusion.2), channel_id=1, source_target_pairs={{0,8},{4,12},{8,16},{12,20},{16,24},{20,28},{1,9},{5,13},{9,17},{1... | collective-permute-start | bytes 1572872 | tf_op jit(solution)/shard_map/ppermute | solution.py:13
  16.0 4.2 %collective-permute-start = (bf16[2,256,512]{1,2,0:T(8,128)(2,1)}, bf16[2,256,512]{1,2,0:T(8,128)(2,1)}, u32[]{:S(2)}, u32[]{:S(2)}) collective-permute-start(bf16[2,256,512]{1,2,0:T(8,128)(2,1)} %pad_maximum_fusion.2), channel_id=1, source_target_pairs={{0,4},{4,8},{8,12},{12,16},{16,20},{20,24},{24,28},{1,5},{5,9},{9,... | collective-permute-start | bytes 1572872 | tf_op jit(solution)/shard_map/ppermute | solution.py:13
  24.6 1.5 select_convert_fusion.2
  29.4 1.5 select_convert_fusion
  32.8 1.5 select_convert_fusion.1
  39.9 1.9 fusion.9
  43.8 2.1 copy.129
  48.1 1.2 fusion.16
  49.3 2.3 fusion.21
  52.7 1.2 copy.121
  54.0 2.1 fusion.69
  56.1 2.0 copy.125
  59.1 2.0 copy.124
  62.2 2.0 copy.128
  64.2 2.3 pad_maximum_fusion.1
  66.6 1.3 collective-permute-start.3
  67.9 1.1 pad_maximum_fusion
  68.9 1.4 collective-permute-start.2
  73.2 111.2 %all-reduce.5.cloned.1.call-done = f32[4,128,128]{1,2,0:T(8,128)} async-done(((f32[4,128,128]{1,2,0:T(8,128)}), f32[4,128,128]{1,2,0:T(8,128)}) %all-reduce.5.cloned.1.call-update) | async-done | bytes 262160 | tf_op jit(solution)/shard_map/psum | solution.py:188
  184.5 1.8 copy.135
  186.3 1.8 fusion.19
  189.0 67.1 %all-reduce.3.cloned.1.call-done = f32[128,512]{1,0:T(8,128)} async-done(((f32[128,512]{1,0:T(8,128)}), f32[128,512]{1,0:T(8,128)}) %all-reduce.3.cloned.1.call-update) | async-done | bytes 262160 | tf_op jit(solution)/shard_map/psum | solution.py:187
  256.1 1.7 copy.163
  (138 shorter events, 27.0 us)
Async XLA Ops:
  8.0 28.2 %copy-start = (bf16[512,512]{1,0:T(8,128)(2,1)S(1)}, bf16[512,512]{1,0:T(8,128)(2,1)}, u32[]{:S(2)}) copy-start(bf16[512,512]{1,0:T(8,128)(2,1)} %param.19) | copy-start | bytes 1572868
  8.0 176.5 %all-reduce.5.cloned.1.call-start = ((), (), s32[]{:S(2)}) async-start(), calls=%async_computation.3 | async-start | bytes 524288 | tf_op jit(solution)/shard_map/psum | solution.py:188
  10.2 18.1 %collective-permute-start.1 = (bf16[2,256,512]{1,2,0:T(8,128)(2,1)}, bf16[2,256,512]{1,2,0:T(8,128)(2,1)}, u32[]{:S(2)}, u32[]{:S(2)}) collective-permute-start(bf16[2,256,512]{1,2,0:T(8,128)(2,1)} %pad_maximum_fusion.2), channel_id=1, source_target_pairs={{0,8},{4,12},{8,16},{12,20},{16,24},{20,28},{1,9},{5,13},{9,17},{1... | collective-permute-start | bytes 1572872 | tf_op jit(solution)/shard_map/ppermute | solution.py:13
  16.0 15.7 %collective-permute-start = (bf16[2,256,512]{1,2,0:T(8,128)(2,1)}, bf16[2,256,512]{1,2,0:T(8,128)(2,1)}, u32[]{:S(2)}, u32[]{:S(2)}) collective-permute-start(bf16[2,256,512]{1,2,0:T(8,128)(2,1)} %pad_maximum_fusion.2), channel_id=1, source_target_pairs={{0,4},{4,8},{8,12},{12,16},{16,20},{20,24},{24,28},{1,5},{5,9},{9,... | collective-permute-start | bytes 1572872 | tf_op jit(solution)/shard_map/ppermute | solution.py:13
  20.2 1.6 copy-start.28
  20.3 5.8 %copy-start.7 = (bf16[256,4,128]{2,1,0:T(4,128)(2,1)}, bf16[256,4,128]{2,1,0:T(4,128)(2,1)S(1)}, u32[]{:S(2)}) copy-start(bf16[256,4,128]{2,1,0:T(4,128)(2,1)S(1)} %reshape_squeeze_stack_squeeze.9) | copy-start | bytes 786436
  20.3 2.7 %copy-start.19 = (bf16[1,256,512]{2,1,0:T(8,128)(2,1)S(1)}, bf16[1,256,512]{2,1,0:T(8,128)(2,1)}, u32[]{:S(2)}) copy-start(bf16[1,256,512]{2,1,0:T(8,128)(2,1)} %param.10) | copy-start | bytes 786436
  23.9 4.1 %copy-start.23 = (s32[1,256]{1,0:T(1,128)}, s32[1,256]{1,0:T(1,128)S(1)}, u32[]{:S(2)}) copy-start(s32[1,256]{1,0:T(1,128)S(1)} %get-tuple-element.40) | copy-start | bytes 3076
  27.4 2.0 copy-start.21
  29.4 1.5 copy-start.10
  29.4 1.5 copy-start.12
  32.8 1.5 copy-start.17
  32.8 1.5 copy-start.14
  39.9 1.9 copy-start.15
  39.9 1.9 copy-start.30
  41.9 1.3 copy-start.29
  43.8 2.1 copy-start.26
  49.3 137.0 %reduce-scatter.2.cloned.1.call-start = ((), (), s32[]{:S(2)}) async-start(), calls=%async_computation.1 | async-start | bytes 1310720 | tf_op jit(solution)/shard_map/reduce_scatter | solution.py:179
  53.9 202.1 %all-reduce.3.cloned.1.call-start = ((), (), s32[]{:S(2)}) async-start(), calls=%async_computation.2 | async-start | bytes 524288 | tf_op jit(solution)/shard_map/psum | solution.py:187
  64.2 3.6 %copy-start.5 = (f32[1,256,512]{2,1,0:T(8,128)S(1)}, f32[1,256,512]{2,1,0:T(8,128)}, u32[]{:S(2)}) copy-start(f32[1,256,512]{2,1,0:T(8,128)} %copy.125) | copy-start | bytes 1572868
  64.2 3.6 %copy-start.6 = (f32[1,256,512]{2,1,0:T(8,128)S(1)}, f32[1,256,512]{2,1,0:T(8,128)}, u32[]{:S(2)}) copy-start(f32[1,256,512]{2,1,0:T(8,128)} %copy.124) | copy-start | bytes 1572868
  66.6 119.8 %collective-permute-start.3 = (f32[2,256,512]{2,1,0:T(8,128)}, f32[2,256,512]{2,1,0:T(8,128)}, u32[]{:S(2)}, u32[]{:S(2)}) collective-permute-start(f32[2,256,512]{2,1,0:T(8,128)} %pad_maximum_fusion.1), channel_id=1, source_target_pairs={{8,0},{12,4},{16,8},{20,12},{24,16},{28,20},{9,1},{13,5},{17,9},{2... | collective-permute-start | bytes 3145736 | tf_op jit(solution)/shard_map/ppermute | solution.py:13
  68.9 1.7 copy-start.11
  68.9 117.4 %collective-permute-start.2 = (f32[2,256,512]{2,1,0:T(8,128)}, f32[2,256,512]{2,1,0:T(8,128)}, u32[]{:S(2)}, u32[]{:S(2)}) collective-permute-start(f32[2,256,512]{2,1,0:T(8,128)} %pad_maximum_fusion), channel_id=1, source_target_pairs={{4,0},{8,4},{12,8},{16,12},{20,16},{24,20},{28,24},{5,1},{9,5},{13... | collective-permute-start | bytes 3145736 | tf_op jit(solution)/shard_map/ppermute | solution.py:13
  (14 other events, 12.8 us)
Sparse Core Ops, SparseCore 0:
  49.4 135.0 all-reduce.4
Sparse Core Ops, SparseCore 1:
  54.0 33.1 reduce-scatter.1
  186.4 69.6 all-reduce.2
where the time goes:
time: 266 us; the launch traced here: 265 us
  waiting for transfers between devices  178 us (67%)
  local copies, waits for them, and re-layouts  25 us (9%)
  matrix products  23.2 us (9%)
  between operations  16.1 us (6%)
  starting transfers between devices  12.8 us (5%)
  other arithmetic  9.79 us (4%)
    psum x1, waiting for transfers between devices, shards(): table_grad = lax.psum(table_local, ('ctx', 'dp'))  111 us
    psum x1, waiting for transfers between devices, shards(): projection_grad = lax.psum(weight_rows, 'ctx')  67.1 us
    ppermute x4, starting transfers between devices, passed_along(): return lax.ppermute(value, axis, pairs)  12.6 us
    unnamed x70, local copies, waits for them, and re-layouts  9.61 us
    another operation x3, local copies, waits for them, and re-layouts, shards(): key_terms.append(jnp.stack([key_part, value_part]))  5.33 us
  transfers between devices with their start and end apart: 7, of which 2 were waited for; matrix products, arithmetic and copies ran while one was open for 13% of the time, Pallas kernels for 0%

commit v1 on v0

--- a/solution.py
+++ b/solution.py
@@ -184,7 +184,7 @@
         scatter_dimension=0,
         tiled=True,
     )
-    projection_grad = lax.psum(weight_rows, "ctx")
+    projection_grad = lax.all_gather(weight_rows, "ctx").sum(axis=0)
     table_grad = lax.psum(table_local, ("ctx", "dp"))
     return (
         query_grad[None],

time: 266 us -> 231 us (0.87)
  waiting for transfers between devices: 178 us -> 143 us
  local copies, waits for them, and re-layouts: 25 us -> 20.7 us
    psum x1 -> x0, waiting for transfers between devices: 67.1 us -> none  [shards(): projection_grad = lax.psum(weight_rows, 'ctx')]
    reduce_scatter x1, waiting for transfers between devices: 0.01 us -> 27.6 us  [shards(): lax.psum_scatter(lax.dot_general(mixed, grad_rows, (((0,), (0,)), ((), ()...]
    unnamed x70 -> x65, local copies, waits for them, and re-layouts: 9.61 us -> 4.71 us
    psum x1, waiting for transfers between devices: 111 us -> 115 us  [shards(): table_grad = lax.psum(table_local, ('ctx', 'dp'))]
  transfers between devices with their start and end apart: 7 -> 7, of which waited for: 2 -> 3; matrix products, arithmetic and copies ran while one was open for 13% -> 19% of each run, Pallas kernels for 0% -> 0%
where the time goes in v1:
time: 231 us; the launch traced here: 230 us
  waiting for transfers between devices  143 us (62%)
  matrix products  25.2 us (11%)
  local copies, waits for them, and re-layouts  20.7 us (9%)
  between operations  16.1 us (7%)
  starting transfers between devices  12.8 us (6%)
  other arithmetic  12.3 us (5%)
    psum x1, waiting for transfers between devices, shards(): table_grad = lax.psum(table_local, ('ctx', 'dp'))  115 us
    reduce_scatter x1, waiting for transfers between devices, shards(): lax.psum_scatter(lax.dot_general(mixed, grad_rows, (((0,), (0,)), ((), ()...  27.6 us
    ppermute x4, starting transfers between devices, passed_along(): return lax.ppermute(value, axis, pairs)  12.6 us
    another operation x3, local copies, waits for them, and re-layouts, shards(): key_terms.append(jnp.stack([key_part, value_part]))  5.33 us
    dot_general x3, matrix products, shards(): jnp.einsum('hij,ihd->jhd', weights, grad_heads, preferred_element_type=jn...  5.16 us
    unnamed x65, local copies, waits for them, and re-layouts  4.71 us
  transfers between devices with their start and end apart: 7, of which 3 were waited for; matrix products, arithmetic and copies ran while one was open for 19% of the time, Pallas kernels for 0%

profile of v1, /device:TPU:0, one launch (start us, length us, event | category | flops | bytes accessed | tf_op | source)
XLA Modules:
  0.0 229.9 jit_solution(11317034584292024249)
XLA Ops:
  8.1 1.2 copy.148
  11.2 5.8 %collective-permute-start.1 = (bf16[2,256,512]{1,2,0:T(8,128)(2,1)}, bf16[2,256,512]{1,2,0:T(8,128)(2,1)}, u32[]{:S(2)}, u32[]{:S(2)}) collective-permute-start(bf16[2,256,512]{1,2,0:T(8,128)(2,1)} %pad_maximum_fusion.2), channel_id=1, source_target_pairs={{0,8},{4,12},{8,16},{12,20},{16,24},{20,28},{1,9},{5,13},{9,17},{1... | collective-permute-start | bytes 1572872 | tf_op jit(solution)/shard_map/ppermute | solution.py:13
  17.0 4.2 %collective-permute-start = (bf16[2,256,512]{1,2,0:T(8,128)(2,1)}, bf16[2,256,512]{1,2,0:T(8,128)(2,1)}, u32[]{:S(2)}, u32[]{:S(2)}) collective-permute-start(bf16[2,256,512]{1,2,0:T(8,128)(2,1)} %pad_maximum_fusion.2), channel_id=1, source_target_pairs={{0,4},{4,8},{8,12},{12,16},{16,20},{20,24},{24,28},{1,5},{5,9},{9,... | collective-permute-start | bytes 1572872 | tf_op jit(solution)/shard_map/ppermute | solution.py:13
  24.9 1.4 select_convert_fusion.2
  29.6 1.6 select_convert_fusion
  32.7 1.5 select_convert_fusion.1
  36.0 1.4 fusion.30
  38.5 2.3 %fusion.21 = f32[512,512]{1,0:T(8,128)} fusion(bf16[256,512]{0,1:T(8,128)(2,1)} %bitcast.224, bf16[1,256,512]{2,1,0:T(8,128)(2,1)} %param.14), kind=kOutput, calls=%fused_computation.57 | convolution fusion | flops 134217728 | bytes 1572864 | tf_op jit(solution)/shard_map/dot_general | solution.py:180
  40.9 1.9 fusion.7
  47.7 27.6 %reduce-scatter.2.cloned.1.call-done = f32[128,512]{1,0:T(8,128)} async-done(((f32[512,512]{1,0:T(8,128)}), f32[128,512]{1,0:T(8,128)}) %reduce-scatter.2.cloned.1.call-update) | async-done | bytes 262160 | tf_op jit(solution)/shard_map/reduce_scatter | solution.py:179
  75.4 2.1 fusion.70
  77.4 2.0 copy.129
  80.5 1.2 copy.121
  81.7 2.1 fusion.69
  83.8 2.1 copy.125
  86.9 2.0 copy.124
  90.0 2.0 copy.128
  92.0 2.4 %pad_maximum_fusion.1 = f32[2,256,512]{2,1,0:T(8,128)} fusion(f32[1,256,512]{2,1,0:T(8,128)} %copy.129, f32[1,256,512]{2,1,0:T(8,128)} %copy.128), kind=kLoop, calls=%fused_computation.41 | loop fusion | flops 262144 | bytes 2097152 | tf_op jit(solution)/shard_map/stack | solution.py:172
  94.4 1.4 collective-permute-start.3
  96.9 1.3 collective-permute-start.2
  100.4 115.1 %all-reduce.2.cloned.1.call-done = f32[4,128,128]{1,2,0:T(8,128)} async-done(((f32[4,128,128]{1,2,0:T(8,128)}), f32[4,128,128]{1,2,0:T(8,128)}) %all-reduce.2.cloned.1.call-update) | async-done | bytes 262160 | tf_op jit(solution)/shard_map/psum | solution.py:188
  215.5 1.8 copy.135
  217.3 1.8 fusion.19
  220.0 2.5 %reduce_sum.83 = f32[128,512]{1,0:T(8,128)} reduce(f32[8,128,512]{2,1,0:T(8,128)} %bitcast.210, f32[]{:T(128)} %constant.165.clone.1), dimensions={0}, to_apply=%region_9.10 | reduce | flops 458752 | bytes 2359300 | tf_op jit(solution)/shard_map/reduce_sum | solution.py:187
  (134 shorter events, 25.1 us)
Async XLA Ops:
  8.0 28.0 %copy-start = (bf16[512,512]{1,0:T(8,128)(2,1)S(1)}, bf16[512,512]{1,0:T(8,128)(2,1)}, u32[]{:S(2)}) copy-start(bf16[512,512]{1,0:T(8,128)(2,1)} %param.19) | copy-start | bytes 1572868
  8.0 13.2 %copy-start.8 = (bf16[1,256,512]{2,1,0:T(8,128)(2,1)S(1)}, bf16[1,256,512]{2,1,0:T(8,128)(2,1)}, u32[]{:S(2)}) copy-start(bf16[1,256,512]{2,1,0:T(8,128)(2,1)} %param.12) | copy-start | bytes 786436
  8.0 14.8 %copy-start.26 = (s32[1,6]{1,0:T(1,128)S(1)}, s32[1,6]{1,0:T(1,128)}, u32[]{:S(2)}) copy-start(s32[1,6]{1,0:T(1,128)} %param.16) | copy-start | bytes 76
  8.0 16.0 %copy-start.17 = (bf16[1,256,512]{2,1,0:T(8,128)(2,1)S(1)}, bf16[1,256,512]{2,1,0:T(8,128)(2,1)}, u32[]{:S(2)}) copy-start(bf16[1,256,512]{2,1,0:T(8,128)(2,1)} %param.10) | copy-start | bytes 786436
  8.0 16.1 %copy-start.25 = (s32[1,2048]{1,0:T(1,128)S(1)}, s32[1,2048]{1,0:T(1,128)}, u32[]{:S(2)}) copy-start(s32[1,2048]{1,0:T(1,128)} %param.15) | copy-start | bytes 24580
  8.1 16.2 %copy-start.18 = (bf16[4,128,128]{2,1,0:T(8,128)(2,1)S(1)}, bf16[4,128,128]{2,1,0:T(8,128)(2,1)}, u32[]{:S(2)}) copy-start(bf16[4,128,128]{2,1,0:T(8,128)(2,1)} %param.18) | copy-start | bytes 393220
  8.1 67.3 %reduce-scatter.2.cloned.1.call-start = ((), (), s32[]{:S(2)}) async-start(), calls=%async_computation.1 | async-start | bytes 1310720 | tf_op jit(solution)/shard_map/reduce_scatter | solution.py:179
  11.2 17.3 %collective-permute-start.1 = (bf16[2,256,512]{1,2,0:T(8,128)(2,1)}, bf16[2,256,512]{1,2,0:T(8,128)(2,1)}, u32[]{:S(2)}, u32[]{:S(2)}) collective-permute-start(bf16[2,256,512]{1,2,0:T(8,128)(2,1)} %pad_maximum_fusion.2), channel_id=1, source_target_pairs={{0,8},{4,12},{8,16},{12,20},{16,24},{20,28},{1,9},{5,13},{9,17},{1... | collective-permute-start | bytes 1572872 | tf_op jit(solution)/shard_map/ppermute | solution.py:13
  17.0 14.6 %collective-permute-start = (bf16[2,256,512]{1,2,0:T(8,128)(2,1)}, bf16[2,256,512]{1,2,0:T(8,128)(2,1)}, u32[]{:S(2)}, u32[]{:S(2)}) collective-permute-start(bf16[2,256,512]{1,2,0:T(8,128)(2,1)} %pad_maximum_fusion.2), channel_id=1, source_target_pairs={{0,4},{4,8},{8,12},{12,16},{16,20},{20,24},{24,28},{1,5},{5,9},{9,... | collective-permute-start | bytes 1572872 | tf_op jit(solution)/shard_map/ppermute | solution.py:13
  21.3 5.0 %copy-start.6 = (bf16[256,4,128]{2,1,0:T(4,128)(2,1)}, bf16[256,4,128]{2,1,0:T(4,128)(2,1)S(1)}, u32[]{:S(2)}) copy-start(bf16[256,4,128]{2,1,0:T(4,128)(2,1)S(1)} %reshape_squeeze_stack_squeeze.9) | copy-start | bytes 786436
  24.2 3.9 %copy-start.21 = (s32[1,256]{1,0:T(1,128)}, s32[1,256]{1,0:T(1,128)S(1)}, u32[]{:S(2)}) copy-start(s32[1,256]{1,0:T(1,128)S(1)} %get-tuple-element.40) | copy-start | bytes 3076
  31.1 3.0 %copy-start.2 = (bf16[4,256,256]{2,1,0:T(8,128)(2,1)}, bf16[4,256,256]{2,1,0:T(8,128)(2,1)S(1)}, u32[]{:S(2)}) copy-start(bf16[4,256,256]{2,1,0:T(8,128)(2,1)S(1)} %get-tuple-element.47) | copy-start | bytes 1572868
  37.4 3.5 %copy-start.7 = (bf16[256,4,128]{2,1,0:T(4,128)(2,1)S(1)}, bf16[256,4,128]{2,1,0:T(4,128)(2,1)}, u32[]{:S(2)}) copy-start(bf16[256,4,128]{2,1,0:T(4,128)(2,1)} %copy-done.6) | copy-start | bytes 786436
  40.8 174.7 %all-reduce.2.cloned.1.call-start = ((), (), s32[]{:S(2)}) async-start(), calls=%async_computation.2 | async-start | bytes 524288 | tf_op jit(solution)/shard_map/psum | solution.py:188
  40.9 2.8 %copy-start.14 = (bf16[1,256,512]{1,2,0:T(8,128)(2,1)S(1)}, bf16[1,256,512]{1,2,0:T(8,128)(2,1)}, u32[]{:S(2)}) copy-start(bf16[1,256,512]{1,2,0:T(8,128)(2,1)} %copy-done.13) | copy-start | bytes 786436
  40.9 2.8 %copy-start.20 = (pred[256,256]{1,0:T(8,128)(4,1)S(1)}, pred[256,256]{1,0:T(8,128)(4,1)}, u32[]{:S(2)}) copy-start(pred[256,256]{1,0:T(8,128)(4,1)} %copy.101) | copy-start | bytes 196612
  40.9 2.8 %copy-start.28 = (f32[4,256,256]{2,1,0:T(8,128)S(1)}, f32[4,256,256]{2,1,0:T(8,128)}, u32[]{:S(2)}) copy-start(f32[4,256,256]{2,1,0:T(8,128)} %get-tuple-element.52) | copy-start | bytes 3145732
  47.7 172.3 %all-gather.3.cloned.1.call-start = ((), (), s32[]{:S(2)}) async-start(), calls=%async_computation.3 | async-start | bytes 2359296 | tf_op jit(solution)/shard_map/all_gather | solution.py:187
  92.0 3.8 %copy-start.4 = (f32[1,256,512]{2,1,0:T(8,128)S(1)}, f32[1,256,512]{2,1,0:T(8,128)}, u32[]{:S(2)}) copy-start(f32[1,256,512]{2,1,0:T(8,128)} %copy.125) | copy-start | bytes 1572868
  92.0 3.8 %copy-start.5 = (f32[1,256,512]{2,1,0:T(8,128)S(1)}, f32[1,256,512]{2,1,0:T(8,128)}, u32[]{:S(2)}) copy-start(f32[1,256,512]{2,1,0:T(8,128)} %copy.124) | copy-start | bytes 1572868
  94.4 4.1 %copy-start.10 = (bf16[1,256,512]{1,2,0:T(8,128)(2,1)S(1)}, bf16[1,256,512]{1,2,0:T(8,128)(2,1)}, u32[]{:S(2)}) copy-start(bf16[1,256,512]{1,2,0:T(8,128)(2,1)} %copy-done.9) | copy-start | bytes 786436
  94.4 4.4 %copy-start.16 = (bf16[1,256,512]{1,2,0:T(8,128)(2,1)S(1)}, bf16[1,256,512]{1,2,0:T(8,128)(2,1)}, u32[]{:S(2)}) copy-start(bf16[1,256,512]{1,2,0:T(8,128)(2,1)} %copy-done.15) | copy-start | bytes 786436
  94.4 122.9 %collective-permute-start.3 = (f32[2,256,512]{2,1,0:T(8,128)}, f32[2,256,512]{2,1,0:T(8,128)}, u32[]{:S(2)}, u32[]{:S(2)}) collective-permute-start(f32[2,256,512]{2,1,0:T(8,128)} %pad_maximum_fusion.1), channel_id=1, source_target_pairs={{8,0},{12,4},{16,8},{20,12},{24,16},{28,20},{9,1},{13,5},{17,9},{2... | collective-permute-start | bytes 3145736 | tf_op jit(solution)/shard_map/ppermute | solution.py:13
  96.9 120.4 %collective-permute-start.2 = (f32[2,256,512]{2,1,0:T(8,128)}, f32[2,256,512]{2,1,0:T(8,128)}, u32[]{:S(2)}, u32[]{:S(2)}) collective-permute-start(f32[2,256,512]{2,1,0:T(8,128)} %pad_maximum_fusion), channel_id=1, source_target_pairs={{4,0},{8,4},{12,8},{16,12},{20,16},{24,20},{28,24},{5,1},{9,5},{13... | collective-permute-start | bytes 3145736 | tf_op jit(solution)/shard_map/ppermute | solution.py:13
  (12 other events, 18.3 us)
Sparse Core Ops, SparseCore 0:
  40.9 34.3 reduce-scatter.1
  77.5 63.5 all-gather.2
Sparse Core Ops, SparseCore 1:
  47.8 167.7 all-reduce.1
